TPU v7x, 128 devices: a whole 4x4x4 slice. The times are simulated.
128 devices in a mesh: req: 16 (over z, x), tp: 8 (over y, core).
Axes of the slice: x: 4, y: 4, z: 4, core: 2. Of those that a mesh axis runs over, the one named last changes fastest.
Arguments:
- tokens: bfloat16 [8192, 3072], P('req', 'tp'), may hold values from -3 to 3
- norm_gain: bfloat16 [3072], P('tp'), may hold values from 0.099609375 to 1.8984375
- w_query: bfloat16 [3072, 3072], P(None, 'tp'), may hold values from -0.3125 to 0.3125
- w_key: bfloat16 [3072, 3072], P(None, 'tp'), may hold values from -0.109375 to 0.109375
- w_value: bfloat16 [3072, 3072], P(None, 'tp'), may hold values from -0.109375 to 0.109375
- w_out: bfloat16 [3072, 3072], P('tp'), may hold values from -0.109375 to 0.109375
- prev_keys: bfloat16 [65536, 3072], P('req', 'tp'), may hold values from -300 to 300
- prev_values: bfloat16 [65536, 3072], P('req', 'tp'), may hold values from -6 to 6
- earlier_lengths: int32 [16, 4], P('req'), may hold values from 1 to 2048, 4096 in all within a row
- new_lengths: int32 [16, 4], P('req'), may hold values from 1 to 256, 512 in all within a row
- page_table: int32 [16, 36], P('req'), may hold values from 0 to 575, as said below
Outputs:
- layer_out: bfloat16 [8192, 3072], P('req', 'tp')
- decode_pool: bfloat16 [288, 8, 128, 1536], P('req', 'tp')
Inputs may be any that keep to these rules, and one draw needn't show every extreme that they name: `page_table`: every value appears exactly once. Among the pages of one index of req, at most 2 share the same value // 18, and in every draw some destination receives exactly 2 of them.
All inputs are finite; a program needn't handle non-finite values.
Results may differ from a plain program's by a relative error of at most 0.0075.
Values may be sent and summed in bfloat16 or wider, within the bound.
No kernel may reach another device: no remote copies, remote signals or barrier semaphores. Data moves between devices by JAX's collectives and lax.ppermute only.
A program may use at most 256 MiB of HBM per device.

v0:
```python
import math
import jax
import jax.numpy as jnp
from jax import lax
from jax.sharding import PartitionSpec as P

HD = 96
HG = 4
PAGE = 128
EPSILON = 1e-05
THETA = 10000.0


def from_partner(value, axis, distance):
    mask = 2**distance
    pairs = [(source, source ^ mask) for source in range(lax.axis_size(axis))]
    return lax.ppermute(value, axis, pairs)


def rotate(values, positions, head_size):
    count = values.shape[0]
    half_size = head_size // 2
    shaped = values.reshape(count, -1, head_size)
    freqs = jnp.exp(-math.log(THETA) * 2.0 * jnp.arange(half_size, dtype=jnp.float32) / head_size)
    angles = positions.astype(jnp.float32)[:, None] * freqs[None, :]
    cosine = jnp.cos(angles)[:, None, :]
    sine = jnp.sin(angles)[:, None, :]
    first = shaped[:, :, :half_size]
    second = shaped[:, :, half_size:]
    turned = jnp.concatenate(
        [first * cosine - second * sine, second * cosine + first * sine], axis=2
    )
    return turned.reshape(count, -1)


def request_ids(lengths, count):
    ends = jnp.cumsum(lengths)
    row_index = jnp.arange(count, dtype=jnp.int32)
    return jnp.sum((row_index[:, None] >= ends[None, :]).astype(jnp.int32), axis=1)


def block_layout(earlier, fresh, count):
    owners = request_ids(fresh, count)
    starts = jnp.cumsum(fresh) - fresh
    onehot = (owners[:, None] == jnp.arange(fresh.shape[0], dtype=jnp.int32)[None, :]).astype(
        jnp.int32
    )
    first_row = jnp.sum(onehot * starts[None, :], axis=1)
    before = jnp.sum(onehot * earlier[None, :], axis=1)
    row_index = jnp.arange(count, dtype=jnp.int32)
    return (owners, before + row_index - first_row)


def visible(earlier, owners, prev_count, count):
    prev_owner = request_ids(earlier, prev_count)
    row_index = jnp.arange(count, dtype=jnp.int32)
    old_part = owners[:, None] == prev_owner[None, :]
    new_part = (owners[:, None] == owners[None, :]) & (row_index[None, :] <= row_index[:, None])
    return jnp.concatenate([old_part, new_part], axis=1)


def order_pair(mine, partner, own_half):
    lower = jnp.where(own_half == 0, mine, partner)
    upper = jnp.where(own_half == 0, partner, mine)
    return jnp.stack([lower, upper], axis=1)


def join_heads(stacked, local_width):
    count, halves, rows_page = (stacked.shape[0], stacked.shape[1], stacked.shape[2])
    split_rows = stacked.reshape(count, halves, rows_page, 2, local_width)
    return split_rows.transpose(0, 2, 3, 1, 4).reshape(count, rows_page, 2 * halves * local_width)


def fill_pool(page_rows, slot_ids, slot_count):
    empty = jnp.zeros((slot_count + 1, page_rows.shape[1], page_rows.shape[2]), jnp.bfloat16)
    return empty.at[slot_ids].set(page_rows)[:slot_count][:, None]


def shards(
    tokens,
    norm_gain,
    w_query,
    w_key,
    w_value,
    w_out,
    prev_keys,
    prev_values,
    earlier_lengths,
    new_lengths,
    page_table,
):
    token_count, local_width = tokens.shape
    full_width = w_query.shape[0]
    widened = tokens.astype(jnp.float32)
    square_sums = lax.psum(jnp.sum(widened * widened, axis=1), "tp")
    scaling = lax.rsqrt(square_sums / full_width + EPSILON)
    normed = (widened * scaling[:, None] * norm_gain.astype(jnp.float32)[None, :]).astype(
        jnp.bfloat16
    )
    fragment = lax.all_gather(normed, "tp", axis=1, tiled=True)
    query_raw, key_raw, value_raw = tuple(
        (
            jnp.dot(fragment, weight, preferred_element_type=jnp.float32)
            for weight in (w_query, w_key, w_value)
        )
    )
    earlier = earlier_lengths[0]
    fresh = new_lengths[0]
    owners, positions = block_layout(earlier, fresh, token_count)
    queries = rotate(query_raw, positions, HD).astype(jnp.bfloat16)
    new_keys = rotate(key_raw, positions, HD).astype(jnp.bfloat16)
    new_values = value_raw.astype(jnp.bfloat16)
    keys_all = jnp.concatenate([prev_keys, new_keys], axis=0)
    values_all = jnp.concatenate([prev_values, new_values], axis=0)
    allowed = visible(earlier, owners, prev_keys.shape[0], token_count)
    heads_here = local_width // HD
    scores = jnp.einsum(
        "qhd,khd->hqk",
        queries.reshape(token_count, heads_here, HD),
        keys_all.reshape(-1, heads_here, HD),
        preferred_element_type=jnp.float32,
    ) * HD ** (-0.5)
    scores = jnp.where(allowed[None, :, :], scores, -1e30)
    row_peak = jnp.max(scores, axis=2, keepdims=True)
    weights = jnp.exp(scores - row_peak)
    totals = jnp.sum(weights, axis=2)
    prob_rows = weights.astype(jnp.bfloat16)
    mixture = jnp.einsum(
        "hqk,khd->qhd",
        prob_rows,
        values_all.reshape(-1, heads_here, HD),
        preferred_element_type=jnp.float32,
    )
    attended = (
        (mixture / totals.T[:, :, None]).astype(jnp.bfloat16).reshape(token_count, local_width)
    )
    projected = jnp.dot(attended, w_out, preferred_element_type=jnp.float32)
    summed = lax.psum_scatter(projected, "tp", scatter_dimension=1, tiled=True)
    layer_out = (tokens.astype(jnp.float32) + summed).astype(jnp.bfloat16)
    page_total = keys_all.shape[0] // PAGE
    page_rows = jnp.concatenate(
        [
            keys_all.reshape(page_total, PAGE, local_width),
            values_all.reshape(page_total, PAGE, local_width),
        ],
        axis=2,
    )
    req_count = lax.axis_size("req")
    halves = lax.axis_size("tp") // HG
    slot_count = page_total // halves
    dest_count = req_count * halves
    capacity = 2 * ((page_total // 2 + dest_count - 1) // dest_count)
    table = page_table[0]
    target = table // slot_count
    slot_ids = table % slot_count
    own_half = lax.axis_index("tp") % halves
    order_index = jnp.arange(page_total, dtype=jnp.int32)
    earlier_mask = order_index[:, None] > order_index[None, :]
    placing = jnp.sum(
        ((target[:, None] == target[None, :]) & earlier_mask).astype(jnp.int32), axis=1
    )
    bucket = target * capacity + placing
    send_rows = (
        jnp.zeros((dest_count * capacity, PAGE, 2 * local_width), jnp.bfloat16)
        .at[bucket]
        .set(page_rows)
    )
    send_slots = jnp.full((dest_count * capacity,), slot_count, jnp.int32).at[bucket].set(slot_ids)
    got_rows, got_slots = (
        lax.all_to_all(send_rows, "req", split_axis=0, concat_axis=0, tiled=True),
        lax.all_to_all(send_slots, "req", split_axis=0, concat_axis=0, tiled=True),
    )
    got_rows = got_rows.reshape(req_count, halves, capacity, PAGE, 2 * local_width)
    got_slots = got_slots.reshape(req_count, halves, capacity)
    mine = lax.dynamic_index_in_dim(got_rows, own_half, 1, keepdims=False).reshape(
        req_count * capacity, PAGE, 2 * local_width
    )
    final_slots = lax.dynamic_index_in_dim(got_slots, own_half, 1, keepdims=False).reshape(-1)
    other = lax.dynamic_index_in_dim(got_rows, 1 - own_half, 1, keepdims=False).reshape(
        req_count * capacity, PAGE, 2 * local_width
    )
    partner = from_partner(other, "tp", 0)
    stacked = order_pair(mine, partner, own_half)
    final_rows = join_heads(stacked, local_width)
    decode_pool = fill_pool(final_rows, final_slots, slot_count)
    return (layer_out, decode_pool)


def solution(mesh):
    placed = (
        P("req", "tp"),
        P("tp"),
        P(None, "tp"),
        P(None, "tp"),
        P(None, "tp"),
        P("tp", None),
        P("req", "tp"),
        P("req", "tp"),
        P("req", None),
        P("req", None),
        P("req", None),
    )
    return jax.shard_map(
        shards,
        mesh=mesh,
        in_specs=placed,
        out_specs=(P("req", "tp"), P("req", "tp", None, None)),
        check_vma=False,
    )
```

profile of v0, /device:TPU:1, one launch (start us, length us, event | category | flops | bytes accessed | tf_op | source)
XLA Modules:
  0.0 441.5 jit_solution(15881802135246873474)
XLA Ops:
  9.2 13.5 %psum.7 = f32[512]{0:T(512)S(1)} all-reduce(f32[512]{0:T(512)S(1)} %fusion.16), channel_id=1, replica_groups=mesh['req'=16,'tp'=8] {'tp'}, use_global_device_ids=true, to_apply=%region_1.0 | all-reduce | flops 512 | bytes 4096 | tf_op jit(solution)/shard_map/psum | solution.py:95
  33.6 21.3 %all-gather.2.cloned.1.call-done = bf16[512,3072]{1,0:T(8,128)(2,1)} async-done(((bf16[512,384]{1,0:T(8,128)(2,1)}), bf16[512,3072]{1,0:T(8,128)(2,1)}) %all-gather.2.cloned.1.call-update) | async-done | bytes 3145744 | tf_op jit(solution)/shard_map/all_gather | solution.py:100
  65.1 5.8 %copy.54 = bf16[4608,384]{0,1:T(8,128)(2,1)} copy(bf16[4608,384]{1,0:T(8,128)(2,1)} %pad_maximum_fusion.2) | data formatting | bytes 7077888 | tf_op jit(solution)/shard_map/concatenate | solution.py:113
  70.9 4.5 %convolution_convert_fusion = bf16[512,384]{1,0:T(8,128)(2,1)S(1)} fusion(bf16[512,3072]{1,0:T(8,128)(2,1)} %all-gather.2.cloned.1.call-done, bf16[3072,384]{1,0:T(8,128)(2,1)} %param.15), kind=kOutput, calls=%fused_computation.20 | convolution fusion | flops 1208156160 | bytes 5898240 | tf_op jit(solution)/shard_map/dot_general | solution.py:103
  75.8 7.1 %pad_maximum_fusion = bf16[36,128,768]{2,1,0:T(8,128)(2,1)} fusion(bf16[36,128,384]{2,1,0:T(8,128)(2,1)S(1)} %bitcast.89, bf16[36,128,384]{2,1,0:T(8,128)(2,1)} %bitcast.90), kind=kLoop, calls=%fused_computation.13 | loop fusion | flops 14155776 | bytes 14155776 | tf_op jit(solution)/shard_map/concatenate | solution.py:141
  82.9 6.0 %broadcast_in_dim.20 = bf16[64,128,768]{2,1,0:T(8,128)(2,1)} broadcast(bf16[]{:T(256)} %constant.76.clone.1), dimensions={} | broadcast | bytes 12582914 | tf_op jit(solution)/shard_map/broadcast_in_dim | solution.py:164
  88.9 22.5 %scatter_fusion = bf16[64,128,768]{2,1,0:T(8,128)(2,1)} fusion(bf16[64,128,768]{2,1,0:T(8,128)(2,1)} %broadcast_in_dim.20, s32[36]{0:T(128)S(1)} %fusion.29, bf16[36,128,768]{2,1,0:T(8,128)(2,1)} %pad_maximum_fusion), kind=kCustom, calls=%fused_computation.1 | custom fusion | bytes 21233808 | tf_op jit(solution)/shard_map/scatter | solution.py:166
  111.4 6.7 %all-to-all-start.1 = ((bf16[64,128,768]{2,1,0:T(8,128)(2,1)}), bf16[64,128,768]{2,1,0:T(8,128)(2,1)}, u32[]{:S(2)}, u32[]{:S(2)}) async-start(bf16[64,128,768]{2,1,0:T(8,128)(2,1)} %scatter_fusion), calls=%async_computation.2 | async-start | bytes 25165824 | tf_op jit(solution)/shard_map/all_to_all | solution.py:170
  118.3 18.6 %fusion = (f32[4,512]{1,0:T(4,128)S(1)}, f32[4,512,4608]{2,1,0:T(8,128)}) fusion(pred[512,4608]{1,0:T(8,128)(4,1)} %pad_add_fusion, bf16[4608,4,96]{0,2,1:T(8,128)(2,1)} %bitcast.94, bf16[512,4,48]{0,2,1:T(8,128)(2,1)S(1)} %get-tuple-element.17, bf16[512,4,48]{0,2,1:T(8,128)(2,1)S(1)} %get-tuple-element.16), kind=kOutput, calls=%fused_computation.5 | convolution fusion | flops 1841035264 | bytes 44048384 | tf_op jit(solution)/shard_map/qhd,khd->hqk/dot_general | solution.py:117
  136.8 5.7 %copy.52 = bf16[4608,384]{0,1:T(8,128)(2,1)} copy(bf16[4608,384]{1,0:T(8,128)(2,1)} %copy-done.1) | data formatting | bytes 7077888 | tf_op jit(solution)/shard_map/concatenate | solution.py:114
  142.6 18.2 %fusion.1 = f32[4,512]{1,0:T(4,128)S(1)} fusion(f32[4,512,4608]{2,1,0:T(8,128)} %get-tuple-element.26, f32[4,512]{1,0:T(4,128)S(1)} %get-tuple-element.25, pred[512,4608]{1,0:T(8,128)(4,1)} %pad_add_fusion), kind=kLoop, calls=%fused_computation.6 | loop fusion | flops 37746688 | bytes 40124416 | tf_op jit(solution)/shard_map/reduce_sum | solution.py:126
  160.8 15.3 %fusion.12 = bf16[512,4,96]{0,2,1:T(8,128)(2,1)S(1)} fusion(bf16[4608,4,96]{0,2,1:T(8,128)(2,1)S(1)} %bitcast.95, f32[4,512,4608]{2,1,0:T(8,128)} %get-tuple-element.26, f32[4,512]{1,0:T(4,128)S(1)} %get-tuple-element.25, pred[512,4608]{1,0:T(8,128)(4,1)S(1)} %copy-done.2, f32[512,4]{0,1:T(4,128)S(1)} %bitcast.100), kind=kOutput, calls=%fused_computation.25 | convolution fusion | flops 1850081280 | bytes 44056576 | tf_op jit(solution)/shard_map/hqk,khd->qhd/dot_general | solution.py:128
  176.2 4.5 %fusion.39 = f32[512,3072]{1,0:T(8,128)} fusion(bf16[512,384]{0,1:T(8,128)(2,1)S(1)} %bitcast.99, bf16[384,3072]{1,0:T(8,128)(2,1)S(1)} %copy-done), kind=kOutput, calls=%fused_computation.83 | convolution fusion | flops 1207959552 | bytes 9043968 | tf_op jit(solution)/shard_map/dot_general | solution.py:137
  180.7 125.3 %all-to-all-done.1 = bf16[64,128,768]{2,1,0:T(8,128)(2,1)} async-done(((bf16[64,128,768]{2,1,0:T(8,128)(2,1)}), bf16[64,128,768]{2,1,0:T(8,128)(2,1)}, u32[]{:S(2)}, u32[]{:S(2)}) %all-to-all-start.1) | async-done | bytes 12582944 | tf_op jit(solution)/shard_map/all_to_all | solution.py:170
  306.0 10.7 %constant_dynamic-slice_fusion = (bf16[16,1,2,128,768]{4,3,2,1,0:T(8,128)(2,1)}, bf16[16,1,2,128,768]{4,3,2,1,0:T(8,128)(2,1)}) fusion(bf16[16,2,2,128,768]{4,3,2,1,0:T(8,128)(2,1)} %bitcast.28, s32[]{:T(128)S(6)} %select_n.86, s32[]{:T(128)S(6)} %select_n.89), kind=kLoop, calls=%fused_computation.63 | loop fusion | bytes 25165832 | tf_op jit(solution)/shard_map/jit(dynamic_index_in_dim)/dynamic_slice | solution.py:175
  323.2 6.0 %all-to-all-done = s32[16,4,1]{1,2,0:T(1,128)S(1)} async-done(((s32[16,4,1]{1,2,0:T(1,128)}), s32[16,4,1]{1,2,0:T(1,128)S(1)}, u32[]{:S(2)}, u32[]{:S(2)}) %all-to-all-start) | async-done | bytes 288 | tf_op jit(solution)/shard_map/all_to_all | solution.py:171
  331.5 10.3 %bitcast_select_fusion.1 = (bf16[32,128,768]{2,1,0:T(8,128)(2,1)}, bf16[32,128,768]{2,1,0:T(8,128)(2,1)}) fusion(bf16[32,128,768]{2,1,0:T(8,128)(2,1)} %collective-permute-done, bf16[16,1,2,128,768]{4,3,2,1,0:T(8,128)(2,1)} %get-tuple-element.14, pred[]{:T(512)S(6)} %eq.75), kind=kLoop, calls=%fused_computation.15 | loop fusion | flops 6291456 | bytes 25165824 | tf_op jit(solution)/shard_map/jit(_where)/select_n | solution.py:63
  341.8 8.7 %copy.58 = bf16[32,128,768]{1,2,0:T(8,128)(2,1)} copy(bf16[32,128,768]{2,1,0:T(8,128)(2,1)} %get-tuple-element.12) | data formatting | bytes 12582912 | tf_op jit(solution)/shard_map/jit(_where)/select_n | solution.py:63
  350.5 8.6 %copy.59 = bf16[32,128,768]{1,2,0:T(8,128)(2,1)} copy(bf16[32,128,768]{2,1,0:T(8,128)(2,1)} %get-tuple-element.13) | data formatting | bytes 12582912 | tf_op jit(solution)/shard_map/jit(_where)/select_n | solution.py:64
  359.1 6.2 %maximum_bitcast_fusion = bf16[32,128,2,2,384]{1,4,2,0,3:T(8,128)(2,1)S(1)} fusion(bf16[32,1,128,2,384]{2,4,3,0,1:T(8,128)(2,1)} %bitcast.92, bf16[32,1,128,2,384]{2,4,3,0,1:T(8,128)(2,1)} %bitcast.91), kind=kLoop, calls=%fused_computation.10 | loop fusion | flops 6291456 | bytes 25165824 | tf_op jit(solution)/shard_map/transpose | solution.py:71
  365.3 5.7 %copy.60 = bf16[32,128,2,2,384]{1,4,3,2,0:T(8,128)(2,1)} copy(bf16[32,128,2,2,384]{1,4,2,0,3:T(8,128)(2,1)S(1)} %maximum_bitcast_fusion) | data formatting | bytes 25165824 | tf_op jit(solution)/shard_map/transpose | solution.py:71
  371.0 16.6 %copy.61 = bf16[32,128,1536]{2,1,0:T(8,128)(2,1)} copy(bf16[32,128,1536]{1,2,0:T(8,128)(2,1)} %bitcast.88) | data formatting | bytes 25165824 | tf_op jit(solution)/shard_map/reshape | solution.py:71
  391.4 36.8 %scatter_fusion.1 = bf16[19,128,1536]{2,1,0:T(8,128)(2,1)} fusion(bf16[19,128,1536]{2,1,0:T(8,128)(2,1)} %broadcast_in_dim.18, s32[32]{0:T(128)S(1)} %fusion.30, bf16[32,128,1536]{2,1,0:T(8,128)(2,1)} %copy.61), kind=kCustom, calls=%fused_computation.2 | custom fusion | bytes 37748864 | tf_op jit(solution)/shard_map/scatter | solution.py:76
  428.1 6.6 %slice_bitcast_fusion = bf16[18,1,128,1536]{3,2,1,0:T(8,128)(2,1)} fusion(bf16[19,128,1536]{2,1,0:T(8,128)(2,1)} %scatter_fusion.1), kind=kLoop, calls=%fused_computation.12 | loop fusion | bytes 14155776
  (60 shorter events, 36.1 us)
Async XLA Ops:
  7.2 169.0 %copy-start = (bf16[384,3072]{1,0:T(8,128)(2,1)S(1)}, bf16[384,3072]{1,0:T(8,128)(2,1)}, u32[]{:S(2)}) copy-start(bf16[384,3072]{1,0:T(8,128)(2,1)} %param.16) | copy-start | bytes 7077892
  7.2 47.7 %all-gather.2.cloned.1.call-start = ((), (), s32[]{:S(2)}) async-start(), calls=%async_computation.3 | async-start | bytes 3538944 | tf_op jit(solution)/shard_map/all_gather | solution.py:100
  54.9 4.2 copy-start.6
  54.9 4.3 copy-start.7
  70.9 4.6 %copy-start.5 = (bf16[4096,384]{1,0:T(8,128)(2,1)S(1)}, bf16[4096,384]{1,0:T(8,128)(2,1)}, u32[]{:S(2)}) copy-start(bf16[4096,384]{1,0:T(8,128)(2,1)} %param.18) | copy-start | bytes 9437188
  75.8 7.1 %copy-start.1 = (bf16[4608,384]{1,0:T(8,128)(2,1)}, bf16[4608,384]{1,0:T(8,128)(2,1)S(1)}, u32[]{:S(2)}) copy-start(bf16[4608,384]{1,0:T(8,128)(2,1)S(1)} %pad_maximum_fusion.1) | copy-start | bytes 10616836
  111.4 194.7 %all-to-all-start.1 = ((bf16[64,128,768]{2,1,0:T(8,128)(2,1)}), bf16[64,128,768]{2,1,0:T(8,128)(2,1)}, u32[]{:S(2)}, u32[]{:S(2)}) async-start(bf16[64,128,768]{2,1,0:T(8,128)(2,1)} %scatter_fusion), calls=%async_computation.2 | async-start | bytes 25165824 | tf_op jit(solution)/shard_map/all_to_all | solution.py:170
  118.0 211.5 %reduce-scatter.2.cloned.1.call-start = ((), (), s32[]{:S(2)}) async-start(), calls=%async_computation.4 | async-start | bytes 7077888 | tf_op jit(solution)/shard_map/reduce_scatter | solution.py:138
  142.6 18.2 %copy-start.2 = (pred[512,4608]{1,0:T(8,128)(4,1)S(1)}, pred[512,4608]{1,0:T(8,128)(4,1)}, u32[]{:S(2)}) copy-start(pred[512,4608]{1,0:T(8,128)(4,1)} %pad_add_fusion) | copy-start | bytes 7077892
  142.6 18.2 %copy-start.3 = (bf16[4608,384]{0,1:T(8,128)(2,1)S(1)}, bf16[4608,384]{0,1:T(8,128)(2,1)}, u32[]{:S(2)}) copy-start(bf16[4608,384]{0,1:T(8,128)(2,1)} %copy.52) | copy-start | bytes 10616836
  306.0 23.5 %copy-start.4 = (bf16[512,384]{1,0:T(8,128)(2,1)S(1)}, bf16[512,384]{1,0:T(8,128)(2,1)}, u32[]{:S(2)}) copy-start(bf16[512,384]{1,0:T(8,128)(2,1)} %param.11) | copy-start | bytes 1179652
  316.7 14.8 %collective-permute-start = (bf16[32,128,768]{2,1,0:T(8,128)(2,1)}, bf16[32,128,768]{2,1,0:T(8,128)(2,1)}, u32[]{:S(2)}, u32[]{:S(2)}) collective-permute-start(bf16[32,128,768]{2,1,0:T(8,128)(2,1)} %bitcast.93), channel_id=1, source_target_pairs={{0,1},{1,0},{2,3},{3,2},{4,5},{5,4},{6,7},{7,6},{8,9},{9,8},{10,11... | collective-permute-start | bytes 18874376 | tf_op jit(solution)/shard_map/ppermute | solution.py:17
  319.5 9.7 %all-to-all-start = ((s32[16,4,1]{1,2,0:T(1,128)}), s32[16,4,1]{1,2,0:T(1,128)S(1)}, u32[]{:S(2)}, u32[]{:S(2)}) async-start(s32[16,4,1]{1,2,0:T(1,128)} %bitcast.23), calls=%async_computation.1 | async-start | bytes 16384 | tf_op jit(solution)/shard_map/all_to_all | solution.py:171
Sparse Core Ops, SparseCore 0:
  24.7 30.1 all-gather.1
  180.8 41.9 reduce-scatter.1
where the time goes:
time: 444 us; the launch traced here: 442 us
  waiting for transfers between devices  153 us (34%)
  local copies, waits for them, and re-layouts  139 us (31%)
  other arithmetic  61.3 us (14%)
  matrix products  48.6 us (11%)
  between operations  14.3 us (3%)
  blocking collectives  13.5 us (3%)
  starting transfers between devices  12 us (3%)
    all_to_all x1, waiting for transfers between devices, shards(): lax.all_to_all(send_rows, 'req', split_axis=0, concat_axis=0, tiled=True)  125 us
    scatter x1, local copies, waits for them, and re-layouts, fill_pool(): return empty.at[slot_ids].set(page_rows)[:slot_count][:, None]  36.8 us
    scatter x1, local copies, waits for them, and re-layouts, shards(): send_rows = jnp.zeros((dest_count * capacity, PAGE, 2 * local_width), jnp...  22.5 us
    all_gather x1, waiting for transfers between devices, shards(): fragment = lax.all_gather(normed, 'tp', axis=1, tiled=True)  21.3 us
    dot_general x1, matrix products, shards(): jnp.einsum('qhd,khd->hqk', queries.reshape(token_count, heads_here, HD),...  18.6 us
    reduce_sum x1, other arithmetic, shards(): totals = jnp.sum(weights, axis=2)  18.2 us
    reshape x1, local copies, waits for them, and re-layouts, join_heads(): split_rows.transpose(0, 2, 3, 1, 4)  16.6 us
    dot_general x1, matrix products, shards(): jnp.einsum('hqk,khd->qhd', prob_rows, values_all.reshape(-1, heads_here,...  15.3 us
  transfers between devices with their start and end apart: 5, of which 3 were waited for; matrix products, arithmetic and copies ran while one was open for 19% of the time, Pallas kernels for 0%

commit v1 on v0

--- a/solution.py
+++ b/solution.py
@@ -97,7 +97,9 @@
     normed = (widened * scaling[:, None] * norm_gain.astype(jnp.float32)[None, :]).astype(
         jnp.bfloat16
     )
-    fragment = lax.all_gather(normed, "tp", axis=1, tiled=True)
+    fragment = jnp.concatenate(
+        lax.all_to_all(jnp.stack([normed for _ in range(lax.axis_size("tp"))], 0), "tp", 0, 0), 1
+    )
     query_raw, key_raw, value_raw = tuple(
         (
             jnp.dot(fragment, weight, preferred_element_type=jnp.float32)

time: 444 us -> 474 us (1.068)
  local copies, waits for them, and re-layouts: 139 us -> 165 us
  starting transfers between devices: 12 us -> 22.1 us
  other arithmetic: 61.3 us -> 54.1 us
    all_to_all x0 -> x1, waiting for transfers between devices: none -> 24.6 us  [shards(): lax.all_to_all(jnp.stack([normed for _ in range(lax.axis_size('tp'))], 0)...]
    all_gather x1 -> x0, waiting for transfers between devices: 21.3 us -> none  [shards(): fragment = lax.all_gather(normed, 'tp', axis=1, tiled=True)]
    reshape x0 -> x3, local copies, waits for them, and re-layouts: none -> 15.5 us  [shards(): jnp.concatenate(lax.all_to_all(jnp.stack([normed for _ in range(lax.axis_...]
    unnamed x17 -> x27, local copies, waits for them, and re-layouts: 6.66 us -> 15.3 us
    all_to_all x0 -> x1, starting transfers between devices: none -> 7.23 us  [shards(): lax.all_to_all(jnp.stack([normed for _ in range(lax.axis_size('tp'))], 0)...]
where the time goes in v1:
time: 474 us; the launch traced here: 471 us
  local copies, waits for them, and re-layouts  165 us (35%)
  waiting for transfers between devices  153 us (32%)
  other arithmetic  54.1 us (11%)
  matrix products  48.6 us (10%)
  starting transfers between devices  22.1 us (5%)
  between operations  14.3 us (3%)
  blocking collectives  13.5 us (3%)
    all_to_all x1, waiting for transfers between devices, shards(): lax.all_to_all(send_rows, 'req', split_axis=0, concat_axis=0, tiled=True)  122 us
    scatter x1, local copies, waits for them, and re-layouts, fill_pool(): return empty.at[slot_ids].set(page_rows)[:slot_count][:, None]  36.8 us
    all_to_all x1, waiting for transfers between devices, shards(): lax.all_to_all(jnp.stack([normed for _ in range(lax.axis_size('tp'))], 0)...  24.6 us
    scatter x1, local copies, waits for them, and re-layouts, shards(): send_rows = jnp.zeros((dest_count * capacity, PAGE, 2 * local_width), jnp...  22.5 us
    dot_general x1, matrix products, shards(): jnp.einsum('qhd,khd->hqk', queries.reshape(token_count, heads_here, HD),...  18.6 us
    reduce_sum x1, other arithmetic, shards(): totals = jnp.sum(weights, axis=2)  18.2 us
    reshape x1, local copies, waits for them, and re-layouts, join_heads(): split_rows.transpose(0, 2, 3, 1, 4)  16.6 us
    reshape x3, local copies, waits for them, and re-layouts, shards(): jnp.concatenate(lax.all_to_all(jnp.stack([normed for _ in range(lax.axis_...  15.5 us
  transfers between devices with their start and end apart: 5, of which 3 were waited for; matrix products, arithmetic and copies ran while one was open for 19% of the time, Pallas kernels for 0%

profile of v1, /device:TPU:1, one launch (start us, length us, event | category | flops | bytes accessed | tf_op | source)
XLA Modules:
  0.0 471.1 jit_solution(8729467039895050697)
XLA Ops:
  9.2 13.5 %psum.7 = f32[512]{0:T(512)S(1)} all-reduce(f32[512]{0:T(512)S(1)} %fusion.16), channel_id=1, replica_groups=mesh['req'=16,'tp'=8] {'tp'}, use_global_device_ids=true, to_apply=%region_1.0 | all-reduce | flops 512 | bytes 4096 | tf_op jit(solution)/shard_map/psum | solution.py:95
  25.8 7.2 %all-to-all-start = ((bf16[8,512,384]{2,1,0:T(8,128)(2,1)}), bf16[8,512,384]{2,1,0:T(8,128)(2,1)}, u32[]{:S(2)}, u32[]{:S(2)}) async-start(bf16[8,512,384]{2,1,0:T(8,128)(2,1)} %stack.8), calls=%async_computation | async-start | bytes 6291456 | tf_op jit(solution)/shard_map/all_to_all | solution.py:101
  46.1 24.6 %all-to-all-done = bf16[8,512,384]{2,1,0:T(8,128)(2,1)} async-done(((bf16[8,512,384]{2,1,0:T(8,128)(2,1)}), bf16[8,512,384]{2,1,0:T(8,128)(2,1)}, u32[]{:S(2)}, u32[]{:S(2)}) %all-to-all-start) | async-done | bytes 3145760 | tf_op jit(solution)/shard_map/all_to_all | solution.py:101
  76.1 5.8 %reshape.323 = bf16[512,3072,1]{1,0,2:T(8,128)(2,1)} reshape(bf16[512,8,384]{2,1,0:T(8,128)(2,1)} %copy.63) | data formatting | bytes 6291456 | tf_op jit(solution)/shard_map/reshape | solution.py:100
  94.5 5.8 %copy.68 = bf16[4608,384]{0,1:T(8,128)(2,1)} copy(bf16[4608,384]{1,0:T(8,128)(2,1)} %pad_maximum_fusion.2) | data formatting | bytes 7077888 | tf_op jit(solution)/shard_map/concatenate | solution.py:115
  105.3 7.1 %pad_maximum_fusion = bf16[36,128,768]{2,1,0:T(8,128)(2,1)} fusion(bf16[36,128,384]{2,1,0:T(8,128)(2,1)S(1)} %bitcast.96, bf16[36,128,384]{2,1,0:T(8,128)(2,1)} %bitcast.97), kind=kLoop, calls=%fused_computation.13 | loop fusion | flops 14155776 | bytes 14155776 | tf_op jit(solution)/shard_map/concatenate | solution.py:143
  112.3 6.0 %broadcast_in_dim.20 = bf16[64,128,768]{2,1,0:T(8,128)(2,1)} broadcast(bf16[]{:T(256)} %constant.76.clone.1), dimensions={} | broadcast | bytes 12582914 | tf_op jit(solution)/shard_map/broadcast_in_dim | solution.py:166
  118.3 22.5 %scatter_fusion = bf16[64,128,768]{2,1,0:T(8,128)(2,1)} fusion(bf16[64,128,768]{2,1,0:T(8,128)(2,1)} %broadcast_in_dim.20, s32[36]{0:T(128)S(1)} %fusion.29, bf16[36,128,768]{2,1,0:T(8,128)(2,1)} %pad_maximum_fusion), kind=kCustom, calls=%fused_computation.1 | custom fusion | bytes 21233808 | tf_op jit(solution)/shard_map/scatter | solution.py:168
  140.8 7.6 %all-to-all-start.2 = ((bf16[64,128,768]{2,1,0:T(8,128)(2,1)}), bf16[64,128,768]{2,1,0:T(8,128)(2,1)}, u32[]{:S(2)}, u32[]{:S(2)}) async-start(bf16[64,128,768]{2,1,0:T(8,128)(2,1)} %scatter_fusion), calls=%async_computation.3 | async-start | bytes 25165824 | tf_op jit(solution)/shard_map/all_to_all | solution.py:172
  148.5 18.6 %fusion = (f32[4,512]{1,0:T(4,128)S(1)}, f32[4,512,4608]{2,1,0:T(8,128)}) fusion(pred[512,4608]{1,0:T(8,128)(4,1)} %pad_add_fusion, bf16[4608,4,96]{0,2,1:T(8,128)(2,1)} %bitcast.101, bf16[512,4,48]{0,2,1:T(8,128)(2,1)S(1)} %get-tuple-element.17, bf16[512,4,48]{0,2,1:T(8,128)(2,1)S(1)} %get-tuple-element.16), kind=kOutput, calls=%fused_computation.5 | convolution fusion | flops 1841035264 | bytes 44048384 | tf_op jit(solution)/shard_map/qhd,khd->hqk/dot_general | solution.py:119
  167.0 5.7 %copy.64 = bf16[4608,384]{0,1:T(8,128)(2,1)} copy(bf16[4608,384]{1,0:T(8,128)(2,1)} %copy-done.1) | data formatting | bytes 7077888 | tf_op jit(solution)/shard_map/concatenate | solution.py:116
  172.8 18.2 %fusion.1 = f32[4,512]{1,0:T(4,128)S(1)} fusion(f32[4,512,4608]{2,1,0:T(8,128)} %get-tuple-element.26, f32[4,512]{1,0:T(4,128)S(1)} %get-tuple-element.25, pred[512,4608]{1,0:T(8,128)(4,1)} %pad_add_fusion), kind=kLoop, calls=%fused_computation.6 | loop fusion | flops 37746688 | bytes 40124416 | tf_op jit(solution)/shard_map/reduce_sum | solution.py:128
  191.0 15.3 %fusion.12 = bf16[512,4,96]{0,2,1:T(8,128)(2,1)S(1)} fusion(bf16[4608,4,96]{0,2,1:T(8,128)(2,1)S(1)} %bitcast.102, f32[4,512,4608]{2,1,0:T(8,128)} %get-tuple-element.26, f32[4,512]{1,0:T(4,128)S(1)} %get-tuple-element.25, pred[512,4608]{1,0:T(8,128)(4,1)S(1)} %copy-done.2, f32[512,4]{0,1:T(4,128)S(1)} %bitcast.108), kind=kOutput, calls=%fused_computation.25 | convolution fusion | flops 1850081280 | bytes 44056576 | tf_op jit(solution)/shard_map/hqk,khd->qhd/dot_general | solution.py:130
  210.9 122.2 %all-to-all-done.2 = bf16[64,128,768]{2,1,0:T(8,128)(2,1)} async-done(((bf16[64,128,768]{2,1,0:T(8,128)(2,1)}), bf16[64,128,768]{2,1,0:T(8,128)(2,1)}, u32[]{:S(2)}, u32[]{:S(2)}) %all-to-all-start.2) | async-done | bytes 12582944 | tf_op jit(solution)/shard_map/all_to_all | solution.py:172
  333.2 10.7 %constant_dynamic-slice_fusion = (bf16[16,1,2,128,768]{4,3,2,1,0:T(8,128)(2,1)}, bf16[16,1,2,128,768]{4,3,2,1,0:T(8,128)(2,1)}) fusion(bf16[16,2,2,128,768]{4,3,2,1,0:T(8,128)(2,1)} %bitcast.31, s32[]{:T(128)S(6)} %select_n.86, s32[]{:T(128)S(6)} %select_n.89), kind=kLoop, calls=%fused_computation.63 | loop fusion | bytes 25165832 | tf_op jit(solution)/shard_map/jit(dynamic_index_in_dim)/dynamic_slice | solution.py:177
  352.5 6.3 %all-to-all-done.1 = s32[16,4,1]{1,2,0:T(1,128)S(1)} async-done(((s32[16,4,1]{1,2,0:T(1,128)}), s32[16,4,1]{1,2,0:T(1,128)S(1)}, u32[]{:S(2)}, u32[]{:S(2)}) %all-to-all-start.1) | async-done | bytes 288 | tf_op jit(solution)/shard_map/all_to_all | solution.py:173
  361.1 10.3 %bitcast_select_fusion.1 = (bf16[32,128,768]{2,1,0:T(8,128)(2,1)}, bf16[32,128,768]{2,1,0:T(8,128)(2,1)}) fusion(bf16[32,128,768]{2,1,0:T(8,128)(2,1)} %collective-permute-done, bf16[16,1,2,128,768]{4,3,2,1,0:T(8,128)(2,1)} %get-tuple-element.14, pred[]{:T(512)S(6)} %eq.75), kind=kLoop, calls=%fused_computation.15 | loop fusion | flops 6291456 | bytes 25165824 | tf_op jit(solution)/shard_map/jit(_where)/select_n | solution.py:63
  371.4 8.7 %copy.72 = bf16[32,128,768]{1,2,0:T(8,128)(2,1)} copy(bf16[32,128,768]{2,1,0:T(8,128)(2,1)} %get-tuple-element.12) | data formatting | bytes 12582912 | tf_op jit(solution)/shard_map/jit(_where)/select_n | solution.py:63
  380.1 8.6 %copy.73 = bf16[32,128,768]{1,2,0:T(8,128)(2,1)} copy(bf16[32,128,768]{2,1,0:T(8,128)(2,1)} %get-tuple-element.13) | data formatting | bytes 12582912 | tf_op jit(solution)/shard_map/jit(_where)/select_n | solution.py:64
  388.7 6.2 %maximum_bitcast_fusion = bf16[32,128,2,2,384]{1,4,2,0,3:T(8,128)(2,1)S(1)} fusion(bf16[32,1,128,2,384]{2,4,3,0,1:T(8,128)(2,1)} %bitcast.99, bf16[32,1,128,2,384]{2,4,3,0,1:T(8,128)(2,1)} %bitcast.98), kind=kLoop, calls=%fused_computation.10 | loop fusion | flops 6291456 | bytes 25165824 | tf_op jit(solution)/shard_map/transpose | solution.py:71
  394.8 5.7 %copy.74 = bf16[32,128,2,2,384]{1,4,3,2,0:T(8,128)(2,1)} copy(bf16[32,128,2,2,384]{1,4,2,0,3:T(8,128)(2,1)S(1)} %maximum_bitcast_fusion) | data formatting | bytes 25165824 | tf_op jit(solution)/shard_map/transpose | solution.py:71
  400.6 16.6 %copy.75 = bf16[32,128,1536]{2,1,0:T(8,128)(2,1)} copy(bf16[32,128,1536]{1,2,0:T(8,128)(2,1)} %bitcast.95) | data formatting | bytes 25165824 | tf_op jit(solution)/shard_map/reshape | solution.py:71
  420.9 36.8 %scatter_fusion.1 = bf16[19,128,1536]{2,1,0:T(8,128)(2,1)} fusion(bf16[19,128,1536]{2,1,0:T(8,128)(2,1)} %broadcast_in_dim.18, s32[32]{0:T(128)S(1)} %fusion.30, bf16[32,128,1536]{2,1,0:T(8,128)(2,1)} %copy.75), kind=kCustom, calls=%fused_computation.2 | custom fusion | bytes 37748864 | tf_op jit(solution)/shard_map/scatter | solution.py:76
  457.7 6.6 %slice_bitcast_fusion = bf16[18,1,128,1536]{3,2,1,0:T(8,128)(2,1)} fusion(bf16[19,128,1536]{2,1,0:T(8,128)(2,1)} %scatter_fusion.1), kind=kLoop, calls=%fused_computation.12 | loop fusion | bytes 14155776
  (73 shorter events, 60.2 us)
Async XLA Ops:
  7.2 199.2 %copy-start = (bf16[384,3072]{1,0:T(8,128)(2,1)S(1)}, bf16[384,3072]{1,0:T(8,128)(2,1)}, u32[]{:S(2)}) copy-start(bf16[384,3072]{1,0:T(8,128)(2,1)} %param.16) | copy-start | bytes 7077892
  7.2 25.8 %copy-start.11 = (s32[1,4]{1,0:T(1,128)S(1)}, s32[1,4]{1,0:T(1,128)}, u32[]{:S(2)}) copy-start(s32[1,4]{1,0:T(1,128)} %param.20) | copy-start | bytes 52
  7.2 26.0 %copy-start.9 = (s32[1,36]{1,0:T(1,128)S(1)}, s32[1,36]{1,0:T(1,128)}, u32[]{:S(2)}) copy-start(s32[1,36]{1,0:T(1,128)} %param.21) | copy-start | bytes 436
  7.2 26.3 %copy-start.10 = (s32[1,4]{1,0:T(1,128)S(1)}, s32[1,4]{1,0:T(1,128)}, u32[]{:S(2)}) copy-start(s32[1,4]{1,0:T(1,128)} %param.19) | copy-start | bytes 52
  25.8 44.9 %all-to-all-start = ((bf16[8,512,384]{2,1,0:T(8,128)(2,1)}), bf16[8,512,384]{2,1,0:T(8,128)(2,1)}, u32[]{:S(2)}, u32[]{:S(2)}) async-start(bf16[8,512,384]{2,1,0:T(8,128)(2,1)} %stack.8), calls=%async_computation | async-start | bytes 6291456 | tf_op jit(solution)/shard_map/all_to_all | solution.py:101
  81.9 4.2 copy-start.7
  81.9 4.3 copy-start.8
  88.1 4.3 copy-start.5
  100.3 4.6 copy-start.6
  105.2 7.1 %copy-start.1 = (bf16[4608,384]{1,0:T(8,128)(2,1)}, bf16[4608,384]{1,0:T(8,128)(2,1)S(1)}, u32[]{:S(2)}) copy-start(bf16[4608,384]{1,0:T(8,128)(2,1)S(1)} %pad_maximum_fusion.1) | copy-start | bytes 10616836
  140.8 192.4 %all-to-all-start.2 = ((bf16[64,128,768]{2,1,0:T(8,128)(2,1)}), bf16[64,128,768]{2,1,0:T(8,128)(2,1)}, u32[]{:S(2)}, u32[]{:S(2)}) async-start(bf16[64,128,768]{2,1,0:T(8,128)(2,1)} %scatter_fusion), calls=%async_computation.3 | async-start | bytes 25165824 | tf_op jit(solution)/shard_map/all_to_all | solution.py:172
  148.4 210.7 %reduce-scatter.2.cloned.1.call-start = ((), (), s32[]{:S(2)}) async-start(), calls=%async_computation.4 | async-start | bytes 7077888 | tf_op jit(solution)/shard_map/reduce_scatter | solution.py:140
  172.8 18.2 %copy-start.2 = (pred[512,4608]{1,0:T(8,128)(4,1)S(1)}, pred[512,4608]{1,0:T(8,128)(4,1)}, u32[]{:S(2)}) copy-start(pred[512,4608]{1,0:T(8,128)(4,1)} %pad_add_fusion) | copy-start | bytes 7077892
  172.8 18.2 %copy-start.3 = (bf16[4608,384]{0,1:T(8,128)(2,1)S(1)}, bf16[4608,384]{0,1:T(8,128)(2,1)}, u32[]{:S(2)}) copy-start(bf16[4608,384]{0,1:T(8,128)(2,1)} %copy.64) | copy-start | bytes 10616836
  333.2 25.9 %copy-start.4 = (bf16[512,384]{1,0:T(8,128)(2,1)S(1)}, bf16[512,384]{1,0:T(8,128)(2,1)}, u32[]{:S(2)}) copy-start(bf16[512,384]{1,0:T(8,128)(2,1)} %param.11) | copy-start | bytes 1179652
  343.9 17.2 %collective-permute-start = (bf16[32,128,768]{2,1,0:T(8,128)(2,1)}, bf16[32,128,768]{2,1,0:T(8,128)(2,1)}, u32[]{:S(2)}, u32[]{:S(2)}) collective-permute-start(bf16[32,128,768]{2,1,0:T(8,128)(2,1)} %bitcast.100), channel_id=1, source_target_pairs={{0,1},{1,0},{2,3},{3,2},{4,5},{5,4},{6,7},{7,6},{8,9},{9,8},{10,11... | collective-permute-start | bytes 18874376 | tf_op jit(solution)/shard_map/ppermute | solution.py:17
  347.3 11.5 %all-to-all-start.1 = ((s32[16,4,1]{1,2,0:T(1,128)}), s32[16,4,1]{1,2,0:T(1,128)S(1)}, u32[]{:S(2)}, u32[]{:S(2)}) async-start(s32[16,4,1]{1,2,0:T(1,128)} %bitcast.26), calls=%async_computation.2 | async-start | bytes 16384 | tf_op jit(solution)/shard_map/all_to_all | solution.py:173
Sparse Core Ops, SparseCore 0:
  211.0 41.9 reduce-scatter.1
